TPU v7x, 512 devices: a whole 4x4x16 slice. The times are simulated.
512 devices in a mesh: band: 16 (over x, y), lon: 32 (over z, core).
Axes of the slice: x: 4, y: 4, z: 16, core: 2. Of those that a mesh axis runs over, the one named last changes fastest.
Arguments:
- sky_maps: float32 [16, 8192, 256], P(None, ('band', 'lon')), may hold values from -9 to 9
- noise_var: float32 [8192, 256], P(('band', 'lon')), may hold values from 1 to 4
- position: float32 [3, 8192, 256], P(None, ('band', 'lon')), may hold values from -1 to 1
- leaf_basis: float32 [8192, 256, 64], P(('band', 'lon')), may hold values from -1 to 1
- leaf_couple: float32 [8192, 4, 64, 64], P(('band', 'lon')), as said below
- transfer: float32 [8192, 64, 64], P(('band', 'lon')), may hold values from -2 to 2
- panel_couple: float32 [1024, 2, 64, 64], P(('band', 'lon')), as said below
- near_list: int32 [8192, 5], P(('band', 'lon')), may hold values from -1 to 8191, as said below
- far_list: int32 [8192, 4], P(('band', 'lon')), may hold values from 0 to 8191, as said below
- panel_list: int32 [1024, 2], P(('band', 'lon')), may hold values from 0 to 1023, as said below
- leaf_panel: int32 [8192], P(('band', 'lon')), may hold values from 0 to 1
Outputs:
- solution: float32 [16, 8192, 256], P(None, ('band', 'lon'))
- residual: float32 [16, 8192, 256], P(None, ('band', 'lon'))
Inputs may be any that keep to these rules, and one draw needn't show every extreme that they name: `near_list`: entry 0 of a row is the leaf itself; the entries after it that are not -1 come first and are distinct leaves of the same band at cycle distance 1 or 2, the cycle closing; leaf j stands in leaf i's row exactly when i stands in j's. `far_list`: distinct leaves of the same band at cycle distance 3 to 6, the cycle closing; leaf j stands in leaf i's row exactly when i stands in j's. If leaf j stands in slot s of far_list[i] and leaf i in slot t of far_list[j], then leaf_couple[j, t] is the transpose of leaf_couple[i, s]. `panel_list`: entries are panel s of sectors of other bands at the same longitude (sector ids differing by a nonzero multiple of the sectors of a band), s being the panel's own index in its sector; panel j stands in panel k's row as often as k stands in j's. If panel j stands in slot s of panel_list[k] and these slots pair up with the slots t of panel_list[j] that hold k, then panel_couple[j, t] is the transpose of panel_couple[k, s].
All inputs are finite; a program needn't handle non-finite values.
Results may differ from a plain program's by a relative error of at most 0.0003.
Values sent between devices are 32-bit elements; how exact they have to be, the bound alone decides.
No kernel may reach another device: no remote copies, remote signals or barrier semaphores. Data moves between devices by JAX's collectives and lax.ppermute only.
A program may use at most 128 MiB of HBM per device.

v0:
```python
import math
import jax
import jax.numpy as jnp
from jax import lax
from jax.sharding import PartitionSpec as P

REACH = 6
ITERS = 2
HIGHEST_PRECISION = lax.Precision.HIGHEST
ROOT_THREE = math.sqrt(3.0)
AMPLITUDE = 0.02


def extended(cells, sides, width):
    for axis, dim in sides:
        count = lax.axis_size(axis)
        head = lax.slice_in_dim(cells, 0, width, axis=dim)
        tail = lax.slice_in_dim(cells, cells.shape[dim] - width, cells.shape[dim], axis=dim)
        cells = jnp.concatenate(
            [
                lax.ppermute(tail, axis, [(i, (i + 1) % count) for i in range(count)]),
                cells,
                lax.ppermute(head, axis, [((i + 1) % count, i) for i in range(count)]),
            ],
            axis=dim,
        )
    return cells


def matern_block(rows_pos, cols_pos, length_scale):
    squared = jnp.zeros((cols_pos.shape[1], rows_pos.shape[1], cols_pos.shape[2]), jnp.float32)
    for component in range(3):
        offset = rows_pos[component][None, :, None] - cols_pos[component][:, None, :]
        squared = squared + offset * offset
    scaled = ROOT_THREE * jnp.sqrt(squared) / length_scale
    return AMPLITUDE * (1.0 + scaled) * jnp.exp(-scaled)


def on_device(
    sky_maps,
    noise_var,
    position,
    leaf_basis,
    leaf_couple,
    transfer,
    panel_couple,
    near_list,
    far_list,
    panel_list,
    leaf_panel,
):
    lon_index = lax.axis_index("lon")
    lon_count = lax.axis_size("lon")
    local_leaves = sky_maps.shape[1]
    pixel_count = sky_maps.shape[2]
    cycle_size = local_leaves * lon_count
    panel_count = panel_couple.shape[0]
    length_scale = 2.0 * math.pi / cycle_size
    first_leaf = lon_index * local_leaves
    near_depth = 2

    def rim_index(leaf_ids, depth):
        return (leaf_ids % cycle_size - first_leaf + depth) % cycle_size

    near_valid = near_list >= 0
    near_rows = rim_index(jnp.where(near_valid, near_list, near_list[:, :1]), near_depth)
    far_rows = rim_index(far_list, REACH)
    rim_pos = extended(position, (("lon", 1),), near_depth)

    def leaf_blocks(inputs):
        rows_pos, rows_index, slot_mask = inputs
        cols_pos = rim_pos[:, rows_index]
        return matern_block(rows_pos, cols_pos, length_scale) * slot_mask[:, None, None]

    near_blocks = lax.map(
        leaf_blocks, (jnp.transpose(position, (1, 0, 2)), near_rows, near_valid.astype(jnp.float32))
    )
    band_slot = panel_list // (lon_count * panel_count)
    gathered_rows = band_slot * panel_count + panel_list % panel_count
    membership = (leaf_panel[:, None] == jnp.arange(panel_count, dtype=jnp.int32)[None, :]).astype(
        jnp.float32
    )

    def square_total(vector):
        return lax.psum(jnp.sum(vector * vector, axis=(1, 2)), ("band", "lon"))

    solution = jnp.zeros_like(sky_maps)
    residual = sky_maps
    direction = sky_maps
    norm_now = square_total(residual)
    for iteration in range(ITERS):
        coeffs = jnp.einsum("lpr,mlp->mlr", leaf_basis, direction, precision=HIGHEST_PRECISION)
        joined = jnp.concatenate([direction, coeffs], axis=2)
        rim_joined = extended(joined, (("lon", 1),), REACH)
        rim_values = rim_joined[
            :, REACH - near_depth : REACH + local_leaves + near_depth, :pixel_count
        ]
        rim_coeffs = rim_joined[:, :, pixel_count:]
        near_part = jnp.einsum(
            "lspq,mlsq->mlp", near_blocks, rim_values[:, near_rows], precision=HIGHEST_PRECISION
        )
        leaf_far = jnp.einsum(
            "lsab,mlsb->mla", leaf_couple, rim_coeffs[:, far_rows], precision=HIGHEST_PRECISION
        )
        upward = jnp.einsum("lab,mla->mlb", transfer, coeffs, precision=HIGHEST_PRECISION)
        panel_coeffs = jnp.einsum("lk,mlb->mkb", membership, upward, precision=HIGHEST_PRECISION)
        band_coeffs = lax.all_gather(panel_coeffs, "band", axis=1, tiled=True)
        panel_far = jnp.einsum(
            "ksab,mksb->mka",
            panel_couple,
            band_coeffs[:, gathered_rows],
            precision=HIGHEST_PRECISION,
        )
        downward = jnp.einsum("lk,mkb->mlb", membership, panel_far, precision=HIGHEST_PRECISION)
        leaf_far = leaf_far + jnp.einsum(
            "lab,mlb->mla", transfer, downward, precision=HIGHEST_PRECISION
        )
        far_part = jnp.einsum("lpr,mlr->mlp", leaf_basis, leaf_far, precision=HIGHEST_PRECISION)
        applied = noise_var[None] * direction + near_part + far_part
        curvature_sum = lax.psum(jnp.sum(direction * applied, axis=(1, 2)), ("band", "lon"))
        step_size = norm_now / curvature_sum
        solution = solution + step_size[:, None, None] * direction
        residual = residual - step_size[:, None, None] * applied
        if iteration + 1 < ITERS:
            norm_next = square_total(residual)
            direction = residual + (norm_next / norm_now)[:, None, None] * direction
            norm_now = norm_next
    return (solution, residual)


def solution(mesh):
    placed = (
        P(None, ("band", "lon"), None),
        P(("band", "lon"), None),
        P(None, ("band", "lon"), None),
        P(("band", "lon"), None, None),
        P(("band", "lon"), None, None, None),
        P(("band", "lon"), None, None),
        P(("band", "lon"), None, None, None),
        P(("band", "lon"), None),
        P(("band", "lon"), None),
        P(("band", "lon"), None),
        P(("band", "lon")),
    )
    return jax.shard_map(
        on_device,
        mesh=mesh,
        in_specs=placed,
        out_specs=(P(None, ("band", "lon"), None), P(None, ("band", "lon"), None)),
        check_vma=False,
    )
```

profile of v0, /device:TPU:1, one launch (start us, length us, event | category | flops | bytes accessed | tf_op | source)
XLA Modules:
  0.0 555.7 jit_solution(6584740147777887504)
XLA Ops:
  1.7 3.0 collective-permute-start.2
  4.7 4.4 collective-permute-start.3
  13.5 3.6 collective-permute-start.1
  20.4 20.6 %all_gather.6 = f32[16,32,64]{2,0,1:T(8,128)} all-gather(f32[16,2,64]{2,0,1:T(8,128)S(1)} %copy.56), channel_id=1, replica_groups=mesh['band'=16,'lon'=32] {'band'}, dimensions={1}, use_global_device_ids=true | all-gather | bytes 139264 | tf_op jit(solution)/shard_map/all_gather | solution.py:107
  46.6 98.0 %while.12 = (s32[]{:T(128)}, f32[16,5,256,256]{3,2,1,0:T(8,128)}, f32[16,3,256]{2,1,0:T(4,128)}, s32[16,5]{1,0:T(8,128)S(1)}, f32[3,20,256]{2,0,1:T(4,128)S(1)},...) while((s32[]{:T(128)}, f32[16,5,256,256]{3,2,1,0:T(8,128)}, f32[16,3,256]{2,1,0:T(4,128)}, ...), condition=%wide.region_3.4_spmd, body=%wide.region_2.3_spmd.sunk | while | flops 4588563 | bytes 1434957 | solution.py:75
  50.1 2.8 multiply_dynamic-update-slice_fusion.2
  56.2 2.8 multiply_dynamic-update-slice_fusion.2
  62.3 2.8 multiply_dynamic-update-slice_fusion.2
  68.4 2.8 multiply_dynamic-update-slice_fusion.2
  74.5 2.8 multiply_dynamic-update-slice_fusion.2
  80.6 2.8 multiply_dynamic-update-slice_fusion.2
  86.7 2.9 multiply_dynamic-update-slice_fusion.2
  92.9 2.8 multiply_dynamic-update-slice_fusion.2
  99.0 2.8 multiply_dynamic-update-slice_fusion.2
  105.1 2.9 multiply_dynamic-update-slice_fusion.2
  111.3 2.8 multiply_dynamic-update-slice_fusion.2
  117.3 2.8 multiply_dynamic-update-slice_fusion.2
  123.5 2.8 multiply_dynamic-update-slice_fusion.2
  129.6 2.9 multiply_dynamic-update-slice_fusion.2
  135.7 2.8 multiply_dynamic-update-slice_fusion.2
  141.8 2.8 multiply_dynamic-update-slice_fusion.2
  146.2 2.5 gather_fusion.2
  148.7 2.9 convolution_bitcast_fusion.9
  155.8 21.5 %fusion.6 = f32[16,16,256]{2,0,1:T(8,128)S(1)} fusion(f32[16,16,5,256]{3,0,2,1:T(8,128)} %bitcast.154, f32[16,5,256,256]{3,2,1,0:T(8,128)} %get-tuple-element.79, f32[16,256]{1,0:T(8,128)S(1)} %copy-done.23, f32[16,16,256]{2,1,0:T(8,128)S(1)} %copy-done.1), kind=kOutput, calls=%fused_computation.28 | convolution fusion | flops 1006764032 | bytes 22822912 | tf_op jit(solution)/shard_map/lspq,mlsq->mlp/dot_general | solution.py:99
  178.1 107.3 %all-reduce = (f32[16]{0:T(128)S(1)}, f32[16]{0:T(128)S(1)}) all-reduce(f32[16]{0:T(128)S(1)} %copy-done.33, f32[16]{0:T(128)S(1)} %get-tuple-element.120), channel_id=1, replica_groups=mesh['band'=16,'lon'=32] {'band','lon'}, use_global_device_ids=true, to_apply=%region_1.2 | all-reduce | flops 32 | bytes 256 | tf_op jit(solution)/shard_map/psum | solution.py:85
  285.7 100.1 %psum.30 = f32[16]{0:T(128)S(1)} all-reduce(f32[16]{0:T(128)S(1)} %multiply_reduce_fusion.1), channel_id=1, replica_groups=mesh['band'=16,'lon'=32] {'band','lon'}, use_global_device_ids=true, to_apply=%region_7.8 | all-reduce | flops 16 | bytes 128 | tf_op jit(solution)/shard_map/psum | solution.py:85
  389.8 17.5 %all_gather.7 = f32[16,32,64]{2,0,1:T(8,128)S(1)} all-gather(f32[16,2,64]{2,0,1:T(8,128)S(1)} %copy.64), channel_id=1, replica_groups=mesh['band'=16,'lon'=32] {'band'}, dimensions={1}, use_global_device_ids=true | all-gather | bytes 139264 | tf_op jit(solution)/shard_map/all_gather | solution.py:107
  409.1 5.9 %collective-permute-start.4 = (f32[16,6,320]{2,0,1:T(8,128)}, f32[16,6,320]{2,0,1:T(8,128)S(1)}, u32[]{:S(2)}, u32[]{:S(2)}) collective-permute-start(f32[16,6,320]{2,0,1:T(8,128)} %get-tuple-element.110), channel_id=1, source_target_pairs={{0,1},{1,2},{2,3},{3,4},{4,5},{5,6},{6,7},{7,8},{8,9},{9,10},{10,1... | collective-permute-start | bytes 368648 | tf_op jit(solution)/shard_map/ppermute | solution.py:21
  417.5 2.7 collective-permute-done.5
  423.2 3.6 convolution_bitcast_fusion.6
  428.6 21.5 %fusion.5 = f32[16,16,256]{2,0,1:T(8,128)S(1)} fusion(f32[16,16,5,256]{3,0,2,1:T(8,128)} %bitcast.153, f32[16,5,256,256]{3,2,1,0:T(8,128)} %get-tuple-element.79, f32[16,16,256]{2,0,1:T(8,128)S(1)} %multiply_add_fusion.1, f32[16,256]{1,0:T(8,128)S(1)} %copy-done.23), kind=kOutput, calls=%fused_computation.26 | convolution fusion | flops 1006764032 | bytes 22822912 | tf_op jit(solution)/shard_map/lspq,mlsq->mlp/dot_general | solution.py:99
  451.8 102.0 %psum.31 = f32[16]{0:T(128)S(1)} all-reduce(f32[16]{0:T(128)S(1)} %get-tuple-element.122), channel_id=1, replica_groups=mesh['band'=16,'lon'=32] {'band','lon'}, use_global_device_ids=true, to_apply=%region_9.10 | all-reduce | flops 16 | bytes 128 | tf_op jit(solution)/shard_map/psum | solution.py:120
  (317 shorter events, 89.7 us)
Async XLA Ops:
  0.6 148.0 %copy-start = (f32[16,4,64,64]{3,2,1,0:T(8,128)S(1)}, f32[16,4,64,64]{3,2,1,0:T(8,128)}, u32[]{:S(2)}) copy-start(f32[16,4,64,64]{3,2,1,0:T(8,128)} %param.17) | copy-start | bytes 3145732
  1.7 43.5 %collective-permute-start.2 = (f32[3,2,256]{2,0,1:T(4,128)S(1)}, f32[3,2,256]{2,0,1:T(4,128)S(1)}, u32[]{:S(2)}, u32[]{:S(2)}) collective-permute-start(f32[3,2,256]{2,0,1:T(4,128)S(1)} %get-tuple-element.116), channel_id=1, source_target_pairs={{0,1},{1,2},{2,3},{3,4},{4,5},{5,6},{6,7},{7,8},{8,9},{9,10},{10,1... | collective-permute-start | bytes 18440 | tf_op jit(solution)/shard_map/ppermute | solution.py:21
  4.7 12.3 %copy-start.1 = (f32[16,16,256]{2,1,0:T(8,128)S(1)}, f32[16,16,256]{2,1,0:T(8,128)}, u32[]{:S(2)}) copy-start(f32[16,16,256]{2,1,0:T(8,128)} %param.13) | copy-start | bytes 786436
  4.7 41.0 %collective-permute-start.3 = (f32[3,2,256]{2,0,1:T(4,128)S(1)}, f32[3,2,256]{2,0,1:T(4,128)}, u32[]{:S(2)}, u32[]{:S(2)}) collective-permute-start(f32[3,2,256]{2,0,1:T(4,128)S(1)} %get-tuple-element.117), channel_id=1, source_target_pairs={{1,0},{2,1},{3,2},{4,3},{5,4},{6,5},{7,6},{8,7},{9,8},{10,9},{11,1... | collective-permute-start | bytes 18440 | tf_op jit(solution)/shard_map/ppermute | solution.py:23
  10.2 7.6 %copy-start.30 = (s32[16,5]{0,1:T(8,128)S(1)}, s32[16,5]{0,1:T(8,128)}, u32[]{:S(2)}) copy-start(s32[16,5]{0,1:T(8,128)} %param.20) | copy-start | bytes 964
  10.3 7.7 %copy-start.32 = (s32[2,2]{1,0:T(2,128)S(1)}, s32[2,2]{1,0:T(2,128)}, u32[]{:S(2)}) copy-start(s32[2,2]{1,0:T(2,128)} %param.22) | copy-start | bytes 52
  10.3 7.8 %copy-start.31 = (s32[16,4]{0,1:T(4,128)S(1)}, s32[16,4]{0,1:T(4,128)}, u32[]{:S(2)}) copy-start(s32[16,4]{0,1:T(4,128)} %param.21) | copy-start | bytes 772
  10.3 9.4 %copy-start.4 = (f32[16,64,64]{2,1,0:T(8,128)S(1)}, f32[16,64,64]{2,1,0:T(8,128)}, u32[]{:S(2)}) copy-start(f32[16,64,64]{2,1,0:T(8,128)} %param.18) | copy-start | bytes 786436
  10.3 9.9 %copy-start.25 = (s32[16]{0:T(128)S(1)}, s32[16]{0:T(128)}, u32[]{:S(2)}) copy-start(s32[16]{0:T(128)} %param.23) | copy-start | bytes 196
  12.7 131.9 %copy-start.7 = (f32[16,16,64]{2,0,1:T(8,128)}, f32[16,16,64]{2,0,1:T(8,128)S(1)}, u32[]{:S(2)}) copy-start(f32[16,16,64]{2,0,1:T(8,128)S(1)} %convolution_bitcast_fusion.11) | copy-start | bytes 196612
  13.5 131.1 %collective-permute-start = (f32[16,6,320]{2,0,1:T(8,128)}, f32[16,6,320]{2,0,1:T(8,128)S(1)}, u32[]{:S(2)}, u32[]{:S(2)}) collective-permute-start(f32[16,6,320]{2,0,1:T(8,128)} %get-tuple-element.112), channel_id=1, source_target_pairs={{0,1},{1,2},{2,3},{3,4},{4,5},{5,6},{6,7},{7,8},{8,9},{9,10},{10,1... | collective-permute-start | bytes 368648 | tf_op jit(solution)/shard_map/ppermute | solution.py:21
  13.5 131.1 %collective-permute-start.1 = (f32[16,6,320]{2,0,1:T(8,128)}, f32[16,6,320]{2,0,1:T(8,128)}, u32[]{:S(2)}, u32[]{:S(2)}) collective-permute-start(f32[16,6,320]{2,0,1:T(8,128)} %get-tuple-element.113), channel_id=1, source_target_pairs={{1,0},{2,1},{3,2},{4,3},{5,4},{6,5},{7,6},{8,7},{9,8},{10,9},{11,1... | collective-permute-start | bytes 368648 | tf_op jit(solution)/shard_map/ppermute | solution.py:23
  18.0 28.6 %copy-start.24 = (s32[1024]{0:T(1024)}, s32[1024]{0:T(1024)S(1)}, u32[]{:S(2)}) copy-start(s32[1024]{0:T(1024)S(1)} %pad_clamp_fusion.1) | copy-start | bytes 12292
  95.7 3.2 copy-start.27
  108.0 3.2 copy-start.27
  138.5 3.2 copy-start.27
  144.6 6.9 %copy-start.11 = (f32[16,6,320]{2,0,1:T(8,128)}, f32[16,6,320]{2,0,1:T(8,128)S(1)}, u32[]{:S(2)}) copy-start(f32[16,6,320]{2,0,1:T(8,128)S(1)} %collective-permute-done) | copy-start | bytes 368644
  148.7 4.5 copy-start.8
  155.8 21.5 %copy-start.2 = (f32[16,256,64]{1,2,0:T(8,128)S(1)}, f32[16,256,64]{1,2,0:T(8,128)}, u32[]{:S(2)}) copy-start(f32[16,256,64]{1,2,0:T(8,128)} %param.16) | copy-start | bytes 3145732
  155.8 21.5 %copy-start.16 = (f32[16,16,64]{2,0,1:T(8,128)S(1)}, f32[16,16,64]{2,0,1:T(8,128)}, u32[]{:S(2)}) copy-start(f32[16,16,64]{2,0,1:T(8,128)} %fusion.8) | copy-start | bytes 196612
  178.1 210.1 %copy-start.5 = (f32[16,16,256]{2,0,1:T(8,128)}, f32[16,16,256]{2,0,1:T(8,128)S(1)}, u32[]{:S(2)}) copy-start(f32[16,16,256]{2,0,1:T(8,128)S(1)} %get-tuple-element.121) | copy-start | bytes 786436
  386.0 3.6 copy-start.26
  388.9 32.8 %copy-start.21 = (s32[1024]{0:T(1024)S(1)}, s32[1024]{0:T(1024)}, u32[]{:S(2)}) copy-start(s32[1024]{0:T(1024)} %pad_clamp_fusion.2) | copy-start | bytes 12292
  409.1 8.3 %collective-permute-start.4 = (f32[16,6,320]{2,0,1:T(8,128)}, f32[16,6,320]{2,0,1:T(8,128)S(1)}, u32[]{:S(2)}, u32[]{:S(2)}) collective-permute-start(f32[16,6,320]{2,0,1:T(8,128)} %get-tuple-element.110), channel_id=1, source_target_pairs={{0,1},{1,2},{2,3},{3,4},{4,5},{5,6},{6,7},{7,8},{8,9},{9,10},{10,1... | collective-permute-start | bytes 368648 | tf_op jit(solution)/shard_map/ppermute | solution.py:21
  415.0 5.1 collective-permute-start.5
  423.2 3.6 copy-start.10
  423.2 3.6 copy-start.13
  423.2 3.6 copy-start.15
  428.6 21.5 %copy-start.18 = (f32[16,16,64]{2,1,0:T(8,128)S(1)}, f32[16,16,64]{2,1,0:T(8,128)}, u32[]{:S(2)}) copy-start(f32[16,16,64]{2,1,0:T(8,128)} %convolution_bitcast_fusion.4) | copy-start | bytes 196612
  428.6 21.5 %copy-start.19 = (f32[16,16,64]{2,1,0:T(8,128)S(1)}, f32[16,16,64]{2,1,0:T(8,128)}, u32[]{:S(2)}) copy-start(f32[16,16,64]{2,1,0:T(8,128)} %convolution_bitcast_fusion.6) | copy-start | bytes 196612
  428.6 22.4 %copy-start.3 = (f32[16,256,64]{1,2,0:T(8,128)S(1)}, f32[16,256,64]{1,2,0:T(8,128)}, u32[]{:S(2)}) copy-start(f32[16,256,64]{1,2,0:T(8,128)} %param.16) | copy-start | bytes 3145732
  450.1 103.7 %copy-start.6 = (f32[16,16,256]{2,0,1:T(8,128)S(1)}, f32[16,16,256]{2,0,1:T(8,128)}, u32[]{:S(2)}) copy-start(f32[16,16,256]{2,0,1:T(8,128)} %copy-done.5) | copy-start | bytes 786436
  (38 other events, 103.1 us)
where the time goes:
time: 558 us; the launch traced here: 556 us
  blocking collectives  347 us (62%)
  local copies, waits for them, and re-layouts  67.1 us (12%)
  matrix products  63.6 us (11%)
  other arithmetic  54.6 us (10%)
  starting transfers between devices  16.9 us (3%)
    psum x2, blocking collectives, square_total(): return lax.psum(jnp.sum(vector * vector, axis=(1, 2)), ('band', 'lon'))  207 us
    psum x1, blocking collectives, on_device(): lax.psum(jnp.sum(direction * applied, axis=(1, 2)), ('band', 'lon'))  102 us
    dynamic_update_slice x16, other arithmetic, on_device(): lax.map(leaf_blocks, (jnp.transpose(position, (1, 0, 2)), near_rows, near...  45.3 us
    dot_general x2, matrix products, on_device(): jnp.einsum('lspq,mlsq->mlp', near_blocks, rim_values[:, near_rows], preci...  42.9 us
    all_gather x2, blocking collectives, on_device(): band_coeffs = lax.all_gather(panel_coeffs, 'band', axis=1, tiled=True)  38 us
    slice x16, local copies, waits for them, and re-layouts, matern_block(): rows_pos[component][None, :, None] - cols_pos[component][:, None, :]  22 us
    mul x16, local copies, waits for them, and re-layouts, leaf_blocks(): matern_block(rows_pos, cols_pos, length_scale) * slot_mask[:, None, None]  20 us
  transfers between devices with their start and end apart: 6, of which 2 were waited for; matrix products, arithmetic and copies ran while one was open for 20% of the time, Pallas kernels for 0%

commit v1 on v0

--- a/solution.py
+++ b/solution.py
@@ -104,7 +104,8 @@
         )
         upward = jnp.einsum("lab,mla->mlb", transfer, coeffs, precision=HIGHEST_PRECISION)
         panel_coeffs = jnp.einsum("lk,mlb->mkb", membership, upward, precision=HIGHEST_PRECISION)
-        band_coeffs = lax.all_gather(panel_coeffs, "band", axis=1, tiled=True)
+        copies = jnp.concatenate([panel_coeffs] * lax.axis_size("band"), axis=1)
+        band_coeffs = lax.all_to_all(copies, "band", 1, 1, tiled=True)
         panel_far = jnp.einsum(
             "ksab,mksb->mka",
             panel_couple,

time: 558 us -> 543 us (0.973)
  blocking collectives: 347 us -> 303 us
  other arithmetic: 54.6 us -> 72.2 us
  starting transfers between devices: 16.9 us -> 23.6 us
    all_gather x2 -> x0, blocking collectives: 38 us -> none  [on_device(): band_coeffs = lax.all_gather(panel_coeffs, 'band', axis=1, tiled=True)]
    select_n x16, other arithmetic: 0.12 us -> 11.1 us  [leaf_blocks(): cols_pos = rim_pos[:, rows_index]]
    slice x16, local copies, waits for them, and re-layouts: 22 us -> 12.7 us  [matern_block(): rows_pos[component][None, :, None] - cols_pos[component][:, None, :]]
    all_to_all x0 -> x2, starting transfers between devices: none -> 8.56 us  [on_device(): band_coeffs = lax.all_to_all(copies, 'band', 1, 1, tiled=True)]
    concatenate x0 -> x4, local copies, waits for them, and re-layouts: none -> 5.63 us  [on_device(): copies = jnp.concatenate([panel_coeffs] * lax.axis_size('band'), axis=1)]
  transfers between devices with their start and end apart: 6 -> 8, of which waited for: 2 -> 1; matrix products, arithmetic and copies ran while one was open for 20% -> 24% of each run, Pallas kernels for 0% -> 0%
where the time goes in v1:
time: 543 us; the launch traced here: 540 us
  blocking collectives  303 us (56%)
  other arithmetic  72.2 us (13%)
  local copies, waits for them, and re-layouts  71.1 us (13%)
  matrix products  64.4 us (12%)
  starting transfers between devices  23.6 us (4%)
    psum x2, blocking collectives, square_total(): return lax.psum(jnp.sum(vector * vector, axis=(1, 2)), ('band', 'lon'))  204 us
    psum x1, blocking collectives, on_device(): lax.psum(jnp.sum(direction * applied, axis=(1, 2)), ('band', 'lon'))  99.5 us
    dynamic_update_slice x16, other arithmetic, on_device(): lax.map(leaf_blocks, (jnp.transpose(position, (1, 0, 2)), near_rows, near...  45 us
    dot_general x2, matrix products, on_device(): jnp.einsum('lspq,mlsq->mlp', near_blocks, rim_values[:, near_rows], preci...  43.1 us
    mul x16, local copies, waits for them, and re-layouts, leaf_blocks(): matern_block(rows_pos, cols_pos, length_scale) * slot_mask[:, None, None]  20.2 us
    slice x16, local copies, waits for them, and re-layouts, matern_block(): rows_pos[component][None, :, None] - cols_pos[component][:, None, :]  12.7 us
    select_n x16, other arithmetic, leaf_blocks(): cols_pos = rim_pos[:, rows_index]  11.1 us
  transfers between devices with their start and end apart: 8, of which 1 were waited for; matrix products, arithmetic and copies ran while one was open for 24% of the time, Pallas kernels for 0%

profile of v1, /device:TPU:1, one launch (start us, length us, event | category | flops | bytes accessed | tf_op | source)
XLA Modules:
  0.0 540.4 jit_solution(11208897973500850381)
XLA Ops:
  1.7 3.0 collective-permute-start.2
  4.7 3.9 collective-permute-start.3
  14.7 4.2 all-to-all-start
  20.5 5.7 %collective-permute-start.1 = (f32[16,6,320]{2,0,1:T(8,128)}, f32[16,6,320]{2,0,1:T(8,128)}, u32[]{:S(2)}, u32[]{:S(2)}) collective-permute-start(f32[16,6,320]{2,0,1:T(8,128)} %get-tuple-element.113), channel_id=1, source_target_pairs={{1,0},{2,1},{3,2},{4,3},{5,4},{6,5},{7,6},{8,7},{9,8},{10,9},{11,1... | collective-permute-start | bytes 368648 | tf_op jit(solution)/shard_map/ppermute | solution.py:23
  31.5 99.0 %while.12 = (s32[]{:T(128)}, f32[16,5,256,256]{3,2,1,0:T(8,128)}, f32[16,3,256]{2,1,0:T(4,128)}, s32[16,5]{1,0:T(8,128)}, f32[3,20,256]{2,0,1:T(4,128)S(1)}, /*i...) while((s32[]{:T(128)}, f32[16,5,256,256]{3,2,1,0:T(8,128)}, f32[16,3,256]{2,1,0:T(4,128)}, ...), condition=%wide.region_3.4_spmd, body=%wide.region_2.3_spmd.sunk | while | flops 4588563 | bytes 1432341 | solution.py:75
  34.9 2.8 multiply_dynamic-update-slice_fusion.2
  41.0 2.8 multiply_dynamic-update-slice_fusion.2
  47.2 2.8 multiply_dynamic-update-slice_fusion.2
  53.4 2.8 multiply_dynamic-update-slice_fusion.2
  59.6 2.8 multiply_dynamic-update-slice_fusion.2
  65.8 2.8 multiply_dynamic-update-slice_fusion.2
  71.9 2.9 multiply_dynamic-update-slice_fusion.2
  78.2 2.8 multiply_dynamic-update-slice_fusion.2
  84.4 2.8 multiply_dynamic-update-slice_fusion.2
  90.5 2.9 multiply_dynamic-update-slice_fusion.2
  96.8 2.8 multiply_dynamic-update-slice_fusion.2
  103.0 2.8 multiply_dynamic-update-slice_fusion.2
  109.2 2.8 multiply_dynamic-update-slice_fusion.2
  115.3 2.8 multiply_dynamic-update-slice_fusion.2
  121.5 2.8 multiply_dynamic-update-slice_fusion.2
  127.7 2.8 multiply_dynamic-update-slice_fusion.2
  143.5 2.9 convolution_bitcast_fusion.9
  150.6 21.6 %fusion.6 = f32[16,16,256]{2,0,1:T(8,128)S(1)} fusion(f32[16,16,5,256]{3,0,2,1:T(8,128)} %bitcast.162, f32[16,5,256,256]{3,2,1,0:T(8,128)} %get-tuple-element.79, f32[16,256]{1,0:T(8,128)S(1)} %copy-done.22, f32[16,16,256]{2,1,0:T(8,128)S(1)} %copy-done.1), kind=kOutput, calls=%fused_computation.28 | convolution fusion | flops 1006764032 | bytes 22822912 | tf_op jit(solution)/shard_map/lspq,mlsq->mlp/dot_general | solution.py:99
  173.1 104.8 %all-reduce = (f32[16]{0:T(128)S(1)}, f32[16]{0:T(128)S(1)}) all-reduce(f32[16]{0:T(128)S(1)} %copy-done.29, f32[16]{0:T(128)S(1)} %get-tuple-element.120), channel_id=1, replica_groups=mesh['band'=16,'lon'=32] {'band','lon'}, use_global_device_ids=true, to_apply=%region_1.2 | all-reduce | flops 32 | bytes 256 | tf_op jit(solution)/shard_map/psum | solution.py:85
  278.2 99.1 %psum.30 = f32[16]{0:T(128)S(1)} all-reduce(f32[16]{0:T(128)S(1)} %multiply_reduce_fusion.1), channel_id=1, replica_groups=mesh['band'=16,'lon'=32] {'band','lon'}, use_global_device_ids=true, to_apply=%region_7.8 | all-reduce | flops 16 | bytes 128 | tf_op jit(solution)/shard_map/psum | solution.py:85
  380.6 2.7 concatenate.27
  386.9 4.4 all-to-all-start.1
  393.7 4.2 all-to-all-done.1
  397.9 2.5 reduce.1
  409.6 3.5 convolution_bitcast_fusion.6
  415.8 21.5 %fusion.5 = f32[16,16,256]{2,0,1:T(8,128)S(1)} fusion(f32[16,16,5,256]{3,0,2,1:T(8,128)} %bitcast.161, f32[16,5,256,256]{3,2,1,0:T(8,128)} %get-tuple-element.79, f32[16,16,256]{2,0,1:T(8,128)S(1)} %multiply_add_fusion.1, f32[16,256]{1,0:T(8,128)S(1)} %copy-done.22), kind=kOutput, calls=%fused_computation.26 | convolution fusion | flops 1006764032 | bytes 22822912 | tf_op jit(solution)/shard_map/lspq,mlsq->mlp/dot_general | solution.py:99
  439.0 99.5 %psum.31 = f32[16]{0:T(128)S(1)} all-reduce(f32[16]{0:T(128)S(1)} %get-tuple-element.122), channel_id=1, replica_groups=mesh['band'=16,'lon'=32] {'band','lon'}, use_global_device_ids=true, to_apply=%region_9.10 | all-reduce | flops 16 | bytes 128 | tf_op jit(solution)/shard_map/psum | solution.py:121
  (260 shorter events, 110.3 us)
Async XLA Ops:
  0.6 142.9 %copy-start = (f32[16,4,64,64]{3,2,1,0:T(8,128)S(1)}, f32[16,4,64,64]{3,2,1,0:T(8,128)}, u32[]{:S(2)}) copy-start(f32[16,4,64,64]{3,2,1,0:T(8,128)} %param.17) | copy-start | bytes 3145732
  0.6 10.3 %copy-start.4 = (f32[16,64,64]{2,1,0:T(8,128)S(1)}, f32[16,64,64]{2,1,0:T(8,128)}, u32[]{:S(2)}) copy-start(f32[16,64,64]{2,1,0:T(8,128)} %param.18) | copy-start | bytes 786436
  0.7 10.9 %copy-start.23 = (s32[16]{0:T(128)S(1)}, s32[16]{0:T(128)}, u32[]{:S(2)}) copy-start(s32[16]{0:T(128)} %param.23) | copy-start | bytes 196
  1.7 6.9 %copy-start.18 = (f32[3,16,256]{2,0,1:T(4,128)}, f32[3,16,256]{2,0,1:T(4,128)S(1)}, u32[]{:S(2)}) copy-start(f32[3,16,256]{2,0,1:T(4,128)S(1)} %copy.106) | copy-start | bytes 147460
  1.7 28.3 %collective-permute-start.2 = (f32[3,2,256]{2,0,1:T(4,128)S(1)}, f32[3,2,256]{2,0,1:T(4,128)S(1)}, u32[]{:S(2)}, u32[]{:S(2)}) collective-permute-start(f32[3,2,256]{2,0,1:T(4,128)S(1)} %get-tuple-element.116), channel_id=1, source_target_pairs={{0,1},{1,2},{2,3},{3,4},{4,5},{5,6},{6,7},{7,8},{8,9},{9,10},{10,1... | collective-permute-start | bytes 18440 | tf_op jit(solution)/shard_map/ppermute | solution.py:21
  4.7 25.9 %collective-permute-start.3 = (f32[3,2,256]{2,0,1:T(4,128)S(1)}, f32[3,2,256]{2,0,1:T(4,128)}, u32[]{:S(2)}, u32[]{:S(2)}) collective-permute-start(f32[3,2,256]{2,0,1:T(4,128)S(1)} %get-tuple-element.117), channel_id=1, source_target_pairs={{1,0},{2,1},{3,2},{4,3},{5,4},{6,5},{7,6},{8,7},{9,8},{10,9},{11,1... | collective-permute-start | bytes 18440 | tf_op jit(solution)/shard_map/ppermute | solution.py:23
  11.0 128.6 %copy-start.7 = (f32[16,16,64]{2,0,1:T(8,128)}, f32[16,16,64]{2,0,1:T(8,128)S(1)}, u32[]{:S(2)}) copy-start(f32[16,16,64]{2,0,1:T(8,128)S(1)} %convolution_bitcast_fusion.11) | copy-start | bytes 196612
  11.0 7.9 %copy-start.1 = (f32[16,16,256]{2,1,0:T(8,128)S(1)}, f32[16,16,256]{2,1,0:T(8,128)}, u32[]{:S(2)}) copy-start(f32[16,16,256]{2,1,0:T(8,128)} %param.13) | copy-start | bytes 786436
  12.0 15.0 %copy-start.26 = (s32[16,5]{0,1:T(8,128)S(1)}, s32[16,5]{0,1:T(8,128)}, u32[]{:S(2)}) copy-start(s32[16,5]{0,1:T(8,128)} %param.20) | copy-start | bytes 964
  12.0 15.1 %copy-start.28 = (s32[2,2]{1,0:T(2,128)S(1)}, s32[2,2]{1,0:T(2,128)}, u32[]{:S(2)}) copy-start(s32[2,2]{1,0:T(2,128)} %param.22) | copy-start | bytes 52
  12.0 15.8 %copy-start.27 = (s32[16,4]{0,1:T(4,128)S(1)}, s32[16,4]{0,1:T(4,128)}, u32[]{:S(2)}) copy-start(s32[16,4]{0,1:T(4,128)} %param.21) | copy-start | bytes 772
  14.7 115.9 %all-to-all-start = ((f32[16,1,2048]{2,1,0:T(1,128)}), f32[16,1,2048]{2,1,0:T(1,128)}, u32[]{:S(2)}, u32[]{:S(2)}) async-start(f32[16,1,2048]{2,1,0:T(1,128)} %reshape.181), calls=%async_computation | async-start | bytes 262144 | tf_op jit(solution)/shard_map/all_to_all | solution.py:108
  19.8 119.8 %collective-permute-start = (f32[16,6,320]{2,0,1:T(8,128)}, f32[16,6,320]{2,0,1:T(8,128)S(1)}, u32[]{:S(2)}, u32[]{:S(2)}) collective-permute-start(f32[16,6,320]{2,0,1:T(8,128)} %get-tuple-element.112), channel_id=1, source_target_pairs={{0,1},{1,2},{2,3},{3,4},{4,5},{5,6},{6,7},{7,8},{8,9},{9,10},{10,1... | collective-permute-start | bytes 368648 | tf_op jit(solution)/shard_map/ppermute | solution.py:21
  20.5 119.0 %collective-permute-start.1 = (f32[16,6,320]{2,0,1:T(8,128)}, f32[16,6,320]{2,0,1:T(8,128)}, u32[]{:S(2)}, u32[]{:S(2)}) collective-permute-start(f32[16,6,320]{2,0,1:T(8,128)} %get-tuple-element.113), channel_id=1, source_target_pairs={{1,0},{2,1},{3,2},{4,3},{5,4},{6,5},{7,6},{8,7},{9,8},{10,9},{11,1... | collective-permute-start | bytes 368648 | tf_op jit(solution)/shard_map/ppermute | solution.py:23
  28.0 113.1 %copy-start.19 = (s32[1024]{0:T(1024)}, s32[1024]{0:T(1024)S(1)}, u32[]{:S(2)}) copy-start(s32[1024]{0:T(1024)S(1)} %pad_clamp_fusion.2) | copy-start | bytes 12292
  139.6 6.8 %copy-start.12 = (f32[16,6,320]{2,0,1:T(8,128)}, f32[16,6,320]{2,0,1:T(8,128)S(1)}, u32[]{:S(2)}) copy-start(f32[16,6,320]{2,0,1:T(8,128)S(1)} %collective-permute-done) | copy-start | bytes 368644
  143.5 2.9 copy-start.16
  143.5 4.5 copy-start.8
  150.6 21.6 %copy-start.2 = (f32[16,256,64]{1,2,0:T(8,128)S(1)}, f32[16,256,64]{1,2,0:T(8,128)}, u32[]{:S(2)}) copy-start(f32[16,256,64]{1,2,0:T(8,128)} %param.16) | copy-start | bytes 3145732
  150.6 21.7 %copy-start.14 = (f32[16,16,64]{2,0,1:T(8,128)S(1)}, f32[16,16,64]{2,0,1:T(8,128)}, u32[]{:S(2)}) copy-start(f32[16,16,64]{2,0,1:T(8,128)} %fusion.8) | copy-start | bytes 196612
  173.1 206.6 %copy-start.5 = (f32[16,16,256]{2,0,1:T(8,128)}, f32[16,16,256]{2,0,1:T(8,128)S(1)}, u32[]{:S(2)}) copy-start(f32[16,16,256]{2,0,1:T(8,128)S(1)} %get-tuple-element.121) | copy-start | bytes 786436
  380.6 10.7 %copy-start.10 = (f32[16,16,64]{2,0,1:T(8,128)S(1)}, f32[16,16,64]{2,0,1:T(8,128)}, u32[]{:S(2)}) copy-start(f32[16,16,64]{2,0,1:T(8,128)} %copy-done.9) | copy-start | bytes 196612
  386.9 11.0 %all-to-all-start.1 = ((f32[16,1,2048]{2,1,0:T(1,128)}), f32[16,1,2048]{2,1,0:T(1,128)}, u32[]{:S(2)}, u32[]{:S(2)}) async-start(f32[16,1,2048]{2,1,0:T(1,128)} %reshape.183), calls=%async_computation.1 | async-start | bytes 262144 | tf_op jit(solution)/shard_map/all_to_all | solution.py:108
  391.3 16.0 %copy-start.20 = (s32[1024]{0:T(1024)S(1)}, s32[1024]{0:T(1024)}, u32[]{:S(2)}) copy-start(s32[1024]{0:T(1024)} %copy-done.19) | copy-start | bytes 12292
  392.1 13.7 %collective-permute-start.4 = (f32[16,6,320]{2,0,1:T(8,128)}, f32[16,6,320]{2,0,1:T(8,128)S(1)}, u32[]{:S(2)}, u32[]{:S(2)}) collective-permute-start(f32[16,6,320]{2,0,1:T(8,128)} %get-tuple-element.110), channel_id=1, source_target_pairs={{0,1},{1,2},{2,3},{3,4},{4,5},{5,6},{6,7},{7,8},{8,9},{9,10},{10,1... | collective-permute-start | bytes 368648 | tf_op jit(solution)/shard_map/ppermute | solution.py:21
  393.7 12.1 %collective-permute-start.5 = (f32[16,6,320]{2,0,1:T(8,128)}, f32[16,6,320]{2,0,1:T(8,128)}, u32[]{:S(2)}, u32[]{:S(2)}) collective-permute-start(f32[16,6,320]{2,0,1:T(8,128)} %get-tuple-element.111), channel_id=1, source_target_pairs={{1,0},{2,1},{3,2},{4,3},{5,4},{6,5},{7,6},{8,7},{9,8},{10,9},{11,1... | collective-permute-start | bytes 368648 | tf_op jit(solution)/shard_map/ppermute | solution.py:23
  405.7 3.9 copy-start.13
  409.6 3.5 copy-start.11
  415.8 21.5 %copy-start.15 = (f32[16,16,64]{2,1,0:T(8,128)S(1)}, f32[16,16,64]{2,1,0:T(8,128)}, u32[]{:S(2)}) copy-start(f32[16,16,64]{2,1,0:T(8,128)} %convolution_bitcast_fusion.4) | copy-start | bytes 196612
  415.8 21.5 %copy-start.17 = (f32[16,16,64]{2,1,0:T(8,128)S(1)}, f32[16,16,64]{2,1,0:T(8,128)}, u32[]{:S(2)}) copy-start(f32[16,16,64]{2,1,0:T(8,128)} %convolution_bitcast_fusion.6) | copy-start | bytes 196612
  415.8 22.4 %copy-start.3 = (f32[16,256,64]{1,2,0:T(8,128)S(1)}, f32[16,256,64]{1,2,0:T(8,128)}, u32[]{:S(2)}) copy-start(f32[16,256,64]{1,2,0:T(8,128)} %param.16) | copy-start | bytes 3145732
  437.3 101.2 %copy-start.6 = (f32[16,16,256]{2,0,1:T(8,128)S(1)}, f32[16,16,256]{2,0,1:T(8,128)}, u32[]{:S(2)}) copy-start(f32[16,16,256]{2,0,1:T(8,128)} %copy-done.5) | copy-start | bytes 786436
  (6 other events, 9.2 us)
